TPU v7x, 128 devices: a whole 4x4x4 slice. The times are simulated.
128 devices in a mesh: rows: 16 (over z, y), owners: 8 (over x, core).
Axes of the slice: x: 4, y: 4, z: 4, core: 2. Of those that a mesh axis runs over, the one named last changes fastest.
Arguments:
- instrument_feature_matrix: bfloat16 [131072, 1024], P(('rows', 'owners')), may hold values from -11 to 11
- partition_prototypes: float32 [1024, 1024], replicated, may hold values from -1.5 to 1.5
- softmax_sharpness_divisor: float32 [1], replicated, may hold values from 8 to 16
- chosen_partition_label: int32 [131072], P(('rows', 'owners')), may hold values from 0 to 1023, as said below
- partition_holder_team: int32 [1024], replicated, may hold values from 0 to 7, as said below
- orthogonal_quantizer_turn: bfloat16 [1024, 1024], replicated, may hold values from -0.1875 to 0.1875
Outputs:
- routed: bfloat16 [524288, 1024], P(('rows', 'owners'))
- new_centroids: float32 [1024, 1024], replicated
Inputs may be any that keep to these rules, and one draw needn't show every extreme that they name: `partition_holder_team`: every owner group owns at least one cluster; the groups own unequal numbers of clusters. `chosen_partition_label`: among the rows of one device at most 512 have clusters of one owner group, and for every index along rows one owner group receives exactly 512 rows from each of the 8 devices of that index.
All inputs are finite; a program needn't handle non-finite values.
Results may differ from a plain program's by a relative error of at most 0.0035.
The roundings to bfloat16 on the way count: a program that leaves them out, or rounds other values in their place, can miss the bound.
Values may be sent and summed in bfloat16 or wider, within the bound.
No kernel may reach another device: no remote copies, remote signals or barrier semaphores. Data moves between devices by JAX's collectives and lax.ppermute only.
A program may use at most 128 MiB of HBM per device.

v0:
```python
import jax
import jax.numpy as jnp
from jax import lax
from jax.sharding import PartitionSpec as P

CAP = 512


PRIOR = 32.0


def shards(
    instrument_feature_matrix,
    partition_prototypes,
    softmax_sharpness_divisor,
    chosen_partition_label,
    partition_holder_team,
    orthogonal_quantizer_turn,
):
    groups = lax.axis_size("owners")
    clusters = partition_prototypes.shape[0]
    width = instrument_feature_matrix.shape[1]
    owner_group = jnp.sum(
        jnp.where(
            chosen_partition_label[:, None] == jnp.arange(clusters, dtype=jnp.int32)[None, :],
            partition_holder_team[None, :],
            0,
        ),
        axis=1,
    )
    onehot = (owner_group[:, None] == jnp.arange(groups, dtype=jnp.int32)[None, :]).astype(
        jnp.int32
    )
    before = jnp.cumsum(onehot, axis=0) - onehot
    rank_in_group = jnp.sum(before * onehot, axis=1)
    slot_index = owner_group * CAP + rank_in_group
    cent_bf = partition_prototypes.astype(jnp.bfloat16)
    prototype_length_squared_term = jnp.sum(partition_prototypes * partition_prototypes, axis=1)
    pairwise_dot_matrix = jnp.dot(
        instrument_feature_matrix, cent_bf.T, preferred_element_type=jnp.float32
    )
    partition_affinity_logits = (
        2.0 * pairwise_dot_matrix - prototype_length_squared_term[None, :]
    ) / softmax_sharpness_divisor[0]
    weights = jax.nn.softmax(partition_affinity_logits, axis=1)
    weights_bf = weights.astype(jnp.bfloat16)
    part_sums = jnp.dot(weights_bf.T, instrument_feature_matrix, preferred_element_type=jnp.float32)
    part_counts = jnp.sum(weights, axis=0)
    total_sums, total_counts = lax.psum((part_sums, part_counts), ("rows", "owners"))
    new_centroids = (total_sums + PRIOR * partition_prototypes) / (total_counts + PRIOR)[:, None]
    residual_vectors = (
        instrument_feature_matrix.astype(jnp.float32)
        - jnp.take(new_centroids, chosen_partition_label, axis=0)
    ).astype(jnp.bfloat16)
    empty = jnp.full((groups * CAP,) + residual_vectors.shape[1:], 0, residual_vectors.dtype)
    routed = jnp.einsum(
        "scd,de->sce",
        lax.all_to_all(
            empty.at[slot_index]
            .set(residual_vectors)
            .reshape((groups, CAP) + residual_vectors.shape[1:]),
            "owners",
            split_axis=0,
            concat_axis=0,
            tiled=True,
        ),
        orthogonal_quantizer_turn,
        preferred_element_type=jnp.float32,
    ).astype(jnp.bfloat16)
    routed = routed.reshape(groups * CAP, width)
    return (routed, new_centroids)


def solution(mesh):
    return jax.shard_map(
        shards,
        mesh=mesh,
        in_specs=(P(("rows", "owners"), None), P(), P(), P(("rows", "owners")), P(), P()),
        out_specs=(P(("rows", "owners"), None), P()),
        check_vma=False,
    )
```

profile of v0, /device:TPU:1, one launch (start us, length us, event | category | flops | bytes accessed | tf_op | source)
XLA Modules:
  0.0 323.4 jit_solution(8552508084817002129)
XLA Ops:
  7.2 0.0 copy-start
  7.2 0.0 all-reduce.2.cloned.1.call-start
  7.2 0.0 copy-start.1
  8.0 2.8 multiply_reduce_fusion
  10.9 0.0 copy-done.1
  10.9 4.0 %fusion.18 = (f32[1024]{0:T(1024)S(1)}, f32[1024,1024]{0,1:T(8,128)S(1)}) fusion(f32[]{:T(128)} %bitcast.31, f32[1024]{0:T(1024)S(1)} %multiply_reduce_fusion, bf16[1024,1024]{1,0:T(8,128)(2,1)} %param.6, f32[1024,1024]{1,0:T(8,128)S(1)} %copy-done.1), kind=kOutput, calls=%fused_computation.37 | convolution fusion | flops 2152725504 | bytes 10493956 | tf_op jit(solution)/shard_map/dot_general | solution.py:39
  14.9 0.0 copy-start.2
  14.9 0.0 copy-start.3
  14.9 0.6 fusion.3
  15.6 1.5 copy-done.2
  17.1 1.0 copy-done.3
  18.0 4.3 %fusion.6 = f32[1024,1024]{1,0:T(8,128)} fusion(bf16[1024,1024]{1,0:T(8,128)(2,1)S(1)} %copy-done.3, f32[1024,1024]{0,1:T(8,128)S(1)} %get-tuple-element.3, f32[1024]{0:T(1024)S(1)} %fusion.3, f32[1024]{0:T(1024)S(1)} %get-tuple-element.2), kind=kOutput, calls=%fused_computation.16 | convolution fusion | flops 2150629376 | bytes 10493952 | tf_op jit(solution)/shard_map/dot_general | solution.py:47
  22.4 0.0 copy-start.4
  22.4 0.0 copy-start.5
  22.4 0.0 all-reduce.2.cloned.1.call-update
  22.4 0.7 copy-done.4
  23.1 0.0 copy-done.5
  23.1 0.8 select_reduce_fusion
  23.9 2.3 reduce-window.6
  26.1 0.3 slice_reduce_fusion
  26.4 0.2 reduce-window.9
  26.6 3.0 fusion.10
  29.5 69.3 %psum.15 = f32[1024]{0:T(1024)S(1)} all-reduce(f32[1024]{0:T(1024)S(1)} %fusion.10), channel_id=1, replica_groups=mesh['rows'=16,'owners'=8] {'rows','owners'}, use_global_device_ids=true, to_apply=%region_9.10 | all-reduce | flops 1024 | bytes 8192 | tf_op jit(solution)/shard_map/psum | solution.py:49
  98.8 0.1 add_bitcast_fusion
  99.0 81.2 %all-reduce.2.cloned.1.call-done = f32[1024,1024]{1,0:T(8,128)} async-done(((f32[1024,1024]{1,0:T(8,128)}), f32[1024,1024]{1,0:T(8,128)}) %all-reduce.2.cloned.1.call-update) | async-done | bytes 4194320 | tf_op jit(solution)/shard_map/psum | solution.py:49
  180.2 6.8 %add_divide_fusion = f32[1024,1024]{1,0:T(8,128)} fusion(f32[1024,1024]{1,0:T(8,128)} %all-reduce.2.cloned.1.call-done, f32[1024,1024]{1,0:T(8,128)} %param.7, f32[1024]{0:T(1024)S(1)} %broadcast_add_fusion), kind=kLoop, calls=%fused_computation.4 | loop fusion | flops 3145728 | bytes 12587008 | tf_op jit(solution)/shard_map/div | solution.py:50
  187.0 20.1 %scatter_custom_fusion = bf16[4096,1024]{1,0:T(8,128)(2,1)} fusion(s32[1024]{0:T(1024)S(1)} %bitcast.37, bf16[]{:T(256)} %constant.11.clone.1, bf16[1024,1024]{1,0:T(8,128)(2,1)} %param.6, f32[]{:T(128)} %constant.37.clone.1, pred[1024]{0:T(1024)(128)(4,1)S(1)} %compare_and_fusion, f32[1024,1024]{1,0:T(8,128)} %add_divide_fusion, s32[1024]{0:T(1024)S(1)} %fusion.16), kind=kCustom, calls=%fused_computation.10 | custom fusion | flops 4194304 | bytes 14685190 | tf_op jit(solution)/shard_map/scatter | solution.py:60
  207.1 98.5 %all_to_all.5 = bf16[8,512,1024]{2,1,0:T(8,128)(2,1)S(1)} all-to-all(bf16[8,512,1024]{2,1,0:T(8,128)(2,1)} %bitcast.33), channel_id=1, replica_groups=mesh['rows'=16,'owners'=8] {'owners'}, dimensions={0} | all-to-all | bytes 16777216 | tf_op jit(solution)/shard_map/all_to_all | solution.py:58
  305.6 0.0 copy-done
  305.6 11.0 %convolution_convert_fusion = bf16[8,512,1024]{2,1,0:T(8,128)(2,1)} fusion(bf16[8,512,1024]{2,1,0:T(8,128)(2,1)S(1)} %all_to_all.5, bf16[1024,1024]{1,0:T(8,128)(2,1)S(1)} %copy-done), kind=kOutput, calls=%fused_computation.2 | convolution fusion | flops 8594128896 | bytes 18874368 | tf_op jit(solution)/shard_map/scd,de->sce/dot_general | solution.py:56
  (7 shorter events, 0.1 us)
Async XLA Ops:
  7.2 298.4 %copy-start = (bf16[1024,1024]{1,0:T(8,128)(2,1)S(1)}, bf16[1024,1024]{1,0:T(8,128)(2,1)}, u32[]{:S(2)}) copy-start(bf16[1024,1024]{1,0:T(8,128)(2,1)} %param.11) | copy-start | bytes 6291460
  7.2 173.1 %all-reduce.2.cloned.1.call-start = ((), (), s32[]{:S(2)}) async-start(), calls=%async_computation.1 | async-start | bytes 8388608 | tf_op jit(solution)/shard_map/psum | solution.py:49
  7.2 3.7 %copy-start.1 = (f32[1024,1024]{1,0:T(8,128)S(1)}, f32[1024,1024]{1,0:T(8,128)}, u32[]{:S(2)}) copy-start(f32[1024,1024]{1,0:T(8,128)} %param.7) | copy-start | bytes 12582916
  14.9 2.1 copy-start.2
  14.9 3.1 copy-start.3
  22.4 0.7 copy-start.4
  22.4 0.7 copy-start.5
Sparse Core Ops, SparseCore 0:
  22.5 157.6 all-reduce.1
where the time goes:
time: 324 us; the launch traced here: 323 us
  blocking collectives  168 us (52%)
  waiting for transfers between devices  81.3 us (25%)
  other arithmetic  36.6 us (11%)
  matrix products  19.4 us (6%)
  between operations  14.9 us (5%)
  local copies, waits for them, and re-layouts  3.45 us (1%)
    all_to_all x1, blocking collectives, shards(): lax.all_to_all(empty.at[slot_index].set(residual_vectors).reshape((groups...  98.5 us
    psum x1, waiting for transfers between devices, shards(): lax.psum((part_sums, part_counts), ('rows', 'owners'))  81.2 us
    psum x1, blocking collectives, shards(): lax.psum((part_sums, part_counts), ('rows', 'owners'))  69.3 us
    scatter x1, other arithmetic, shards(): routed = jnp.einsum('scd,de->sce', lax.all_to_all(empty.at[slot_index].se...  20.1 us
    dot_general x1, matrix products, shards(): jnp.einsum('scd,de->sce', lax.all_to_all(empty.at[slot_index].set(residua...  11 us
    div x1, other arithmetic, shards(): (total_sums + PRIOR * partition_prototypes) / (total_counts + PRIOR)[:, N...  6.79 us
  transfers between devices with their start and end apart: 1, of which 1 were waited for; matrix products, arithmetic and copies ran while one was open for 2% of the time, Pallas kernels for 0%

commit v1 on v0

v1 whole, which is shorter than its diff:
```python
import jax
import jax.numpy as jnp
from jax import lax
from jax.sharding import PartitionSpec as P

CAP = 512


PRIOR = 32.0


def shards(
    instrument_feature_matrix,
    partition_prototypes,
    softmax_sharpness_divisor,
    chosen_partition_label,
    partition_holder_team,
    orthogonal_quantizer_turn,
):
    groups = lax.axis_size("owners")
    clusters, width = partition_prototypes.shape
    rows = instrument_feature_matrix.shape[0]
    x = instrument_feature_matrix
    labels = chosen_partition_label

    cent_bf = partition_prototypes.astype(jnp.bfloat16)
    prototype_length_squared_term = jnp.sum(partition_prototypes * partition_prototypes, axis=1)
    pairwise_dot_matrix = jnp.dot(x, cent_bf.T, preferred_element_type=jnp.float32)
    partition_affinity_logits = (
        2.0 * pairwise_dot_matrix - prototype_length_squared_term[None, :]
    ) / softmax_sharpness_divisor[0]
    weights = jax.nn.softmax(partition_affinity_logits, axis=1)
    weights_bf = weights.astype(jnp.bfloat16)
    part_sums = jnp.dot(weights_bf.T, x, preferred_element_type=jnp.float32)
    part_counts = jnp.sum(weights, axis=0)
    pad = (-(clusters + 1)) % 8
    packed = jnp.concatenate(
        [part_sums, part_counts.reshape(1, width), jnp.zeros((pad, width), jnp.float32)], axis=0
    )
    total = lax.psum(packed, ("rows", "owners"))

    owner_group = jnp.take(partition_holder_team, labels, axis=0)
    onehot = (owner_group[:, None] == jnp.arange(groups, dtype=jnp.int32)[None, :]).astype(jnp.int32)
    before = jnp.cumsum(onehot, axis=0) - onehot
    rank_in_group = jnp.sum(before * onehot, axis=1)
    slot_index = owner_group * CAP + rank_in_group
    source_row = (
        jnp.full((groups * CAP,), -1, jnp.int32).at[slot_index].set(jnp.arange(rows, dtype=jnp.int32))
    )
    filled = source_row >= 0
    safe_row = jnp.where(filled, source_row, 0)
    slot_x = jnp.take(x, safe_row, axis=0)
    slot_label = jnp.where(filled, jnp.take(labels, safe_row, axis=0), -1)
    recv_x = lax.all_to_all(
        slot_x.reshape(groups, CAP, width), "owners", split_axis=0, concat_axis=0, tiled=True
    ).reshape(groups * CAP, width)
    recv_label = lax.all_to_all(
        slot_label.reshape(groups, CAP), "owners", split_axis=0, concat_axis=0, tiled=True
    ).reshape(groups * CAP)

    total_sums = total[:clusters]
    total_counts = total[clusters]
    new_centroids = (total_sums + PRIOR * partition_prototypes) / (total_counts + PRIOR)[:, None]

    valid = recv_label >= 0
    picked = jnp.take(new_centroids, jnp.where(valid, recv_label, 0), axis=0)
    residual_vectors = (recv_x.astype(jnp.float32) - picked).astype(jnp.bfloat16)
    rotated = jnp.dot(
        residual_vectors, orthogonal_quantizer_turn, preferred_element_type=jnp.float32
    ).astype(jnp.bfloat16)
    routed = jnp.where(valid[:, None], rotated, jnp.zeros_like(rotated))
    return (routed, new_centroids)


def solution(mesh):
    return jax.shard_map(
        shards,
        mesh=mesh,
        in_specs=(P(("rows", "owners"), None), P(), P(), P(("rows", "owners")), P(), P()),
        out_specs=(P(("rows", "owners"), None), P()),
        check_vma=False,
    )
```

time: 324 us -> 336 us (1.037)
  blocking collectives: 168 us -> 0 us
  waiting for transfers between devices: 81.3 us -> 181 us
  local copies, waits for them, and re-layouts: 3.45 us -> 80.6 us
  other arithmetic: 36.6 us -> 23 us
  starting transfers between devices: 0.04 us -> 11 us
  matrix products: 19.4 us -> 23.8 us
    psum x1, waiting for transfers between devices: 81.2 us -> 181 us  [shards(): total = lax.psum(packed, ('rows', 'owners'))]
    all_to_all x1 -> x0, blocking collectives: 98.5 us -> none  [shards(): lax.all_to_all(empty.at[slot_index].set(residual_vectors).reshape((groups...]
    psum x1 -> x0, blocking collectives: 69.3 us -> none  [shards(): lax.psum((part_sums, part_counts), ('rows', 'owners'))]
    gather x0 -> x4, local copies, waits for them, and re-layouts: none -> 65.2 us  [the longest x1 24.6 us: shards(): picked = jnp.take(new_centroids, jnp.where(valid, recv_label, 0), axis=0)]
    scatter x1 -> x0, other arithmetic: 20.1 us -> none  [shards(): routed = jnp.einsum('scd,de->sce', lax.all_to_all(empty.at[slot_index].se...]
    all_to_all x0 -> x2, starting transfers between devices: none -> 10.7 us  [the longest x1 5.79 us: shards(): lax.all_to_all(slot_label.reshape(groups, CAP), 'owners', split_axis=0, c...]
    concatenate x0 -> x1, local copies, waits for them, and re-layouts: none -> 10.7 us  [shards(): jnp.concatenate([part_sums, part_counts.reshape(1, width), jnp.zeros((pad...]
    select_n x1 -> x5, other arithmetic: 0.01 us -> 8 us  [the longest x1 7.34 us: shards(): slot_x = jnp.take(x, safe_row, axis=0)]
  transfers between devices with their start and end apart: 1 -> 3, of which waited for: 1 -> 1; matrix products, arithmetic and copies ran while one was open for 2% -> 24% of each run, Pallas kernels for 0% -> 0%
where the time goes in v1:
time: 336 us; the launch traced here: 335 us
  waiting for transfers between devices  181 us (54%)
  local copies, waits for them, and re-layouts  80.6 us (24%)
  matrix products  23.8 us (7%)
  other arithmetic  23 us (7%)
  between operations  15 us (4%)
  starting transfers between devices  11 us (3%)
    psum x1, waiting for transfers between devices, shards(): total = lax.psum(packed, ('rows', 'owners'))  181 us
    gather x1, local copies, waits for them, and re-layouts, shards(): picked = jnp.take(new_centroids, jnp.where(valid, recv_label, 0), axis=0)  24.6 us
    gather x1, local copies, waits for them, and re-layouts, shards(): slot_x = jnp.take(x, safe_row, axis=0)  18.1 us
    dot_general x1, matrix products, shards(): jnp.dot(residual_vectors, orthogonal_quantizer_turn, preferred_element_ty...  17 us
    gather x1, local copies, waits for them, and re-layouts, shards(): slot_label = jnp.where(filled, jnp.take(labels, safe_row, axis=0), -1)  16.7 us
    concatenate x1, local copies, waits for them, and re-layouts, shards(): jnp.concatenate([part_sums, part_counts.reshape(1, width), jnp.zeros((pad...  10.7 us
    select_n x1, other arithmetic, shards(): slot_x = jnp.take(x, safe_row, axis=0)  7.34 us
    div x1, other arithmetic, shards(): (total_sums + PRIOR * partition_prototypes) / (total_counts + PRIOR)[:, N...  6.78 us
  transfers between devices with their start and end apart: 3, of which 1 were waited for; matrix products, arithmetic and copies ran while one was open for 24% of the time, Pallas kernels for 0%

profile of v1, /device:TPU:1, one launch (start us, length us, event | category | flops | bytes accessed | tf_op | source)
XLA Modules:
  0.0 334.9 jit_solution(6707980680749088741)
XLA Ops:
  7.2 0.0 copy-start
  7.2 0.0 copy-start.2
  7.2 0.8 fusion.22
  8.0 5.7 %gather_fusion = s32[1024]{0:T(1024)S(1)} fusion(s32[1024]{0:T(1024)} %param.10, s32[1024]{0:T(1024)S(1)} %fusion.22), kind=kCustom, calls=%fused_computation | custom fusion | bytes 12288 | tf_op jit(solution)/shard_map/jit(_take)/gather | solution.py:42
  13.8 0.0 copy-done.2
  13.8 2.3 reduce-window.6
  16.1 0.3 slice_reduce_fusion
  16.4 0.2 reduce-window.9
  16.5 0.1 add_bitcast_fusion
  16.6 4.3 %scatter_custom_fusion = s32[4096]{0:T(1024)S(1)} fusion(s32[1024]{0:T(1024)S(1)} %compare_select_fusion.6, s32[1024]{0:T(1024)S(1)} %iota.11, s32[]{:T(128)} %constant.34.clone.1), kind=kCustom, calls=%fused_computation.45 | custom fusion | bytes 16388 | tf_op jit(solution)/shard_map/scatter | solution.py:48
  21.0 16.7 %gather_fusion.1 = s32[4096]{0:T(1024)S(1)} fusion(s32[1024]{0:T(1024)S(1)} %copy-done.2, s32[4096]{0:T(1024)S(1)} %fusion.19), kind=kCustom, calls=%fused_computation.1 | custom fusion | bytes 49152 | tf_op jit(solution)/shard_map/jit(_take)/gather | solution.py:53
  37.7 0.6 compare_select_fusion.4
  38.3 5.8 %all-to-all-start = ((s32[8,1,512]{2,1,0:T(1,128)}), s32[8,1,512]{2,1,0:T(1,128)S(1)}, u32[]{:S(2)}, u32[]{:S(2)}) async-start(s32[8,1,512]{2,1,0:T(1,128)} %bitcast.2), calls=%async_computation | async-start | bytes 32768 | tf_op jit(solution)/shard_map/all_to_all | solution.py:57
  44.1 0.0 copy-done
  44.1 18.1 %gather_fusion.2 = bf16[4096,1024]{1,0:T(8,128)(2,1)} fusion(bf16[1024,1024]{1,0:T(8,128)(2,1)S(1)} %copy-done, s32[4096]{0:T(1024)S(1)} %fusion.19), kind=kCustom, calls=%fused_computation.2 | custom fusion | bytes 16793600 | tf_op jit(solution)/shard_map/jit(_take)/gather | solution.py:52
  62.3 7.3 %broadcast_select_fusion = bf16[8,512,1024]{2,1,0:T(8,128)(2,1)} fusion(bf16[8,512,1024]{2,1,0:T(8,128)(2,1)} %bitcast.35, pred[8,512]{1,0:T(8,128)(4,1)S(1)} %broadcast_in_dim.73), kind=kLoop, calls=%fused_computation.11 | loop fusion | flops 4194304 | bytes 16781312 | tf_op jit(solution)/shard_map/jit(_take)/select_n | solution.py:52
  69.6 0.0 all-to-all-done
  69.6 5.0 %all-to-all-start.1 = ((bf16[8,512,1024]{2,1,0:T(8,128)(2,1)}), bf16[8,512,1024]{2,1,0:T(8,128)(2,1)}, u32[]{:S(2)}, u32[]{:S(2)}) async-start(bf16[8,512,1024]{2,1,0:T(8,128)(2,1)} %broadcast_select_fusion), calls=%async_computation.1 | async-start | bytes 16777216 | tf_op jit(solution)/shard_map/all_to_all | solution.py:54
  74.6 0.2 all-reduce.2.cloned.1.call-start
  74.8 0.0 copy-start.3
  75.6 2.7 multiply_reduce_fusion
  78.3 0.0 copy-done.3
  78.4 2.4 fusion.24
  80.8 0.6 fusion.9
  81.4 0.8 fusion.13
  82.2 4.4 %fusion.10 = f32[1024,1024]{1,0:T(8,128)} fusion(bf16[1024,1024]{1,0:T(8,128)(2,1)S(1)} %copy-done, f32[1024,1024]{0,1:T(8,128)S(1)} %get-tuple-element.5, f32[1024]{0:T(1024)S(1)} %fusion.9, f32[1024]{0:T(1024)S(1)} %get-tuple-element.4), kind=kOutput, calls=%fused_computation.19 | convolution fusion | flops 2150629376 | bytes 10493952 | tf_op jit(solution)/shard_map/dot_general | solution.py:34
  86.5 10.7 %concatenate.3 = f32[1032,1024]{1,0:T(8,128)} concatenate(f32[1024,1024]{1,0:T(8,128)} %fusion.10, f32[1,1024]{1,0:T(1,128)S(1)} %bitcast.40, f32[7,1024]{1,0:T(8,128)S(1)} %broadcast_in_dim.77), dimensions={0} | concatenate | bytes 8454144 | tf_op jit(solution)/shard_map/concatenate | solution.py:37
  97.3 0.0 all-reduce.2.cloned.1.call-update
  97.4 181.4 %all-reduce.2.cloned.1.call-done = f32[1032,1024]{1,0:T(8,128)} async-done(((f32[1032,1024]{1,0:T(8,128)}), f32[1032,1024]{1,0:T(8,128)}) %all-reduce.2.cloned.1.call-update) | async-done | bytes 4227088 | tf_op jit(solution)/shard_map/psum | solution.py:40
  278.8 0.8 slice_add_fusion.1
  279.6 6.8 %fusion.7 = f32[1024,1024]{1,0:T(8,128)} fusion(f32[1032,1024]{1,0:T(8,128)} %all-reduce.2.cloned.1.call-done, f32[1024,1024]{1,0:T(8,128)} %param.7, f32[1024]{0:T(1024)S(1)} %bitcast.41), kind=kLoop, calls=%fused_computation.13 | loop fusion | flops 3145728 | bytes 12587008 | tf_op jit(solution)/shard_map/div | solution.py:63
  286.4 24.6 %gather_fusion.3 = f32[4096,1024]{1,0:T(8,128)} fusion(f32[1024,1024]{1,0:T(8,128)} %fusion.7, s32[4096]{0:T(1024)S(1)} %broadcast_clamp_fusion), kind=kCustom, calls=%fused_computation.3 | custom fusion | bytes 33570816 | tf_op jit(solution)/shard_map/jit(_take)/gather | solution.py:66
  311.0 0.0 all-to-all-done.1
  311.0 0.0 copy-start.1
  311.0 17.0 %convert_select_fusion = bf16[4096,1024]{1,0:T(8,128)(2,1)} fusion(pred[4096]{0:T(1024)(128)(4,1)S(1)} %get-tuple-element.3, bf16[1024,1024]{1,0:T(8,128)(2,1)} %param.11, bf16[4096,1024]{1,0:T(8,128)(2,1)} %bitcast.11, f32[4096,1024]{1,0:T(8,128)} %gather_fusion.3, pred[4096]{0:T(1024)(128)(4,1)S(1)} %get-tuple-element.2), kind=kOutput, calls=%fused_computation.8 | convolution fusion | flops 8615100416 | bytes 35659776 | tf_op jit(solution)/shard_map/dot_general | solution.py:68
  328.0 0.0 copy-done.1
  (12 shorter events, 0.1 us)
Async XLA Ops:
  7.2 37.0 %copy-start = (bf16[1024,1024]{1,0:T(8,128)(2,1)S(1)}, bf16[1024,1024]{1,0:T(8,128)(2,1)}, u32[]{:S(2)}) copy-start(bf16[1024,1024]{1,0:T(8,128)(2,1)} %param.6) | copy-start | bytes 6291460
  7.2 6.6 %copy-start.2 = (s32[1024]{0:T(1024)S(1)}, s32[1024]{0:T(1024)}, u32[]{:S(2)}) copy-start(s32[1024]{0:T(1024)} %param.9) | copy-start | bytes 12292
  38.3 31.3 %all-to-all-start = ((s32[8,1,512]{2,1,0:T(1,128)}), s32[8,1,512]{2,1,0:T(1,128)S(1)}, u32[]{:S(2)}, u32[]{:S(2)}) async-start(s32[8,1,512]{2,1,0:T(1,128)} %bitcast.2), calls=%async_computation | async-start | bytes 32768 | tf_op jit(solution)/shard_map/all_to_all | solution.py:57
  69.6 241.4 %all-to-all-start.1 = ((bf16[8,512,1024]{2,1,0:T(8,128)(2,1)}), bf16[8,512,1024]{2,1,0:T(8,128)(2,1)}, u32[]{:S(2)}, u32[]{:S(2)}) async-start(bf16[8,512,1024]{2,1,0:T(8,128)(2,1)} %broadcast_select_fusion), calls=%async_computation.1 | async-start | bytes 16777216 | tf_op jit(solution)/shard_map/all_to_all | solution.py:54
  74.6 204.2 %all-reduce.2.cloned.1.call-start = ((), (), s32[]{:S(2)}) async-start(), calls=%async_computation.2 | async-start | bytes 8454144 | tf_op jit(solution)/shard_map/psum | solution.py:40
  74.8 3.5 %copy-start.3 = (f32[1024,1024]{1,0:T(8,128)S(1)}, f32[1024,1024]{1,0:T(8,128)}, u32[]{:S(2)}) copy-start(f32[1024,1024]{1,0:T(8,128)} %param.7) | copy-start | bytes 12582916
  311.0 17.0 %copy-start.1 = (bf16[1024,1024]{1,0:T(8,128)(2,1)S(1)}, bf16[1024,1024]{1,0:T(8,128)(2,1)}, u32[]{:S(2)}) copy-start(bf16[1024,1024]{1,0:T(8,128)(2,1)} %param.6) | copy-start | bytes 6291460
Sparse Core Ops, SparseCore 0:
  97.4 181.3 all-reduce.1
